TPU v7x, 32 devices: a whole 2x2x4 slice. The times are simulated.
32 devices in a mesh: fsdp: 8 (over y, x, core), dp: 4 (over z).
Axes of the slice: x: 2, y: 2, z: 4, core: 2. Of those that a mesh axis runs over, the one named last changes fastest.
Arguments:
- tokens: bfloat16 [131072, 1024], P(('fsdp', 'dp')), may hold values from -6 to 6
- cotangent: bfloat16 [131072, 1024], P(('fsdp', 'dp')), may hold values from -6 to 6
- lengths: int32 [256], P(('fsdp', 'dp')), may hold values from 8 to 2048, as said below
- selected: int32 [16384], P(('fsdp', 'dp')), may hold values from 0 to 4095, as said below
- attn_in: bfloat16 [1024, 3072], P('fsdp'), may hold values from -0.1875 to 0.1875
- attn_out: bfloat16 [1024, 1024], P('fsdp'), may hold values from -0.75 to 0.75
- mlp_in: bfloat16 [1024, 4096], P('fsdp'), may hold values from -0.1875 to 0.1875
- mlp_out: bfloat16 [4096, 1024], P('fsdp'), may hold values from -0.09375 to 0.09375
- norm_attn: bfloat16 [1024], P('fsdp'), may hold values from 0.5 to 1.5
- norm_mlp: bfloat16 [1024], P('fsdp'), may hold values from 0.5 to 1.5
- router: bfloat16 [1024], replicated, may hold values from -0.1875 to 0.1875
Outputs:
- output: bfloat16 [131072, 1024], P(('fsdp', 'dp'))
- grad_tokens: bfloat16 [131072, 1024], P(('fsdp', 'dp'))
- grad_attn_in: float32 [1024, 3072], P('fsdp')
- grad_attn_out: float32 [1024, 1024], P('fsdp')
- grad_mlp_in: float32 [1024, 4096], P('fsdp')
- grad_mlp_out: float32 [4096, 1024], P('fsdp')
- grad_norm_attn: float32 [1024], P('fsdp')
- grad_norm_mlp: float32 [1024], P('fsdp')
- grad_router: float32 [1024], replicated
Inputs may be any that keep to these rules, and one draw needn't show every extreme that they name: `lengths`: each aligned block of 8 entries (one device's sequences, in order) holds multiples of 8 that sum to 4096; exactly one of them equals 2048. `selected`: each aligned block of 512 entries lists distinct positions within its device's 4096 tokens in ascending order; a sequence of length L has exactly L / 8 of its positions listed.
All inputs are finite; a program needn't handle non-finite values.
Results may differ from a plain program's by a relative error of at most 0.014.
Values may be sent and summed in bfloat16 or wider, within the bound.
No kernel may reach another device: no remote copies, remote signals or barrier semaphores. Data moves between devices by JAX's collectives and lax.ppermute only.
A program may use at most 192 MiB of HBM per device.

v0:
```python
import jax
import jax.numpy as jnp
from jax import lax
from jax.sharding import PartitionSpec as P

HEADS = 16
HEAD = 64
EPS = 1e-06
MASKED = -1e30


def rms_scale(values, gain_vec):
    return values * lax.rsqrt(jnp.mean(values * values, axis=-1, keepdims=True) + EPS) * gain_vec


def seq_mask(lengths, selected):
    seq_ends = jnp.cumsum(lengths)
    owner_seq = jnp.sum((selected[:, None] >= seq_ends[None, :]).astype(jnp.int32), axis=1)
    return (owner_seq[:, None] == owner_seq[None, :]) & (selected[None, :] <= selected[:, None])


def split_heads(matrix):
    return matrix.reshape(matrix.shape[0], HEADS, HEAD)


def masked_scores(query_heads, key_heads, allowed, score_scale):
    scores = (
        jnp.einsum("qhd,khd->hqk", query_heads, key_heads, preferred_element_type=jnp.float32)
        * score_scale
    )
    return jnp.where(allowed[None], scores, MASKED)


def per_device(
    tokens,
    cotangent,
    lengths,
    selected,
    attn_in,
    attn_out,
    mlp_in,
    mlp_out,
    norm_attn,
    norm_mlp,
    router,
):
    model_width = tokens.shape[1]
    row_count = selected.shape[0]
    score_scale = HEAD ** (-0.5)
    w_qkv, w_out, gain_attn, gain_mlp = (
        lax.all_gather(attn_in, "fsdp", axis=0, tiled=True),
        lax.all_gather(attn_out, "fsdp", axis=0, tiled=True),
        lax.all_gather(norm_attn, "fsdp", axis=0, tiled=True),
        lax.all_gather(norm_mlp, "fsdp", axis=0, tiled=True),
    )
    w_in, w_down = (
        lax.all_gather(mlp_in, "fsdp", axis=0, tiled=True),
        lax.all_gather(mlp_out, "fsdp", axis=0, tiled=True),
    )
    gain_one = gain_attn.astype(jnp.float32)
    gain_two = gain_mlp.astype(jnp.float32)
    positions = lax.broadcasted_iota(jnp.int32, (row_count, tokens.shape[0]), 1)
    select = (selected[:, None] == positions).astype(jnp.bfloat16)
    routed = jnp.dot(select, tokens, preferred_element_type=jnp.float32)
    routed_low = routed.astype(jnp.bfloat16)
    router_rate = jnp.dot(routed_low, router, preferred_element_type=jnp.float32)
    allowed = seq_mask(lengths, selected)
    normed_float, norm_pull = jax.vjp(rms_scale, routed, gain_one)
    normed = normed_float.astype(jnp.bfloat16)
    qkv = jnp.dot(normed, w_qkv, preferred_element_type=jnp.float32).astype(jnp.bfloat16)
    query_heads = split_heads(qkv[:, :model_width])
    key_heads = split_heads(qkv[:, model_width : 2 * model_width])
    value_heads = split_heads(qkv[:, 2 * model_width :])
    scores = masked_scores(query_heads, key_heads, allowed, score_scale)
    highest = jnp.max(scores, axis=-1, keepdims=True)
    exponent = jnp.exp(scores - highest)
    row_total = jnp.sum(exponent, axis=-1, keepdims=True)
    probabilities = (exponent / row_total).astype(jnp.bfloat16)
    log_total = highest + jnp.log(row_total)
    attn_mix = jnp.einsum(
        "hqk,khd->qhd", probabilities, value_heads, preferred_element_type=jnp.float32
    )
    attn_mix = attn_mix.reshape(row_count, model_width).astype(jnp.bfloat16)
    attended = jnp.dot(attn_mix, w_out, preferred_element_type=jnp.float32)
    middle = routed + attended
    normed_two_float, middle_pull = jax.vjp(rms_scale, middle, gain_two)
    normed_two = normed_two_float.astype(jnp.bfloat16)
    pre_gelu = jnp.dot(normed_two, w_in, preferred_element_type=jnp.float32)
    active_float, gelu_pull = jax.vjp(jax.nn.gelu, pre_gelu)
    active = active_float.astype(jnp.bfloat16)
    expanded = jnp.dot(active, w_down, preferred_element_type=jnp.float32)
    update = attended + expanded
    branch = (router_rate[:, None] * update).astype(jnp.bfloat16)
    output = (
        tokens.astype(jnp.float32)
        + jnp.einsum("kt,kd->td", select, branch, preferred_element_type=jnp.float32)
    ).astype(jnp.bfloat16)
    w_qkv_back, w_out_back = (
        lax.all_gather(attn_in, "fsdp", axis=0, tiled=True),
        lax.all_gather(attn_out, "fsdp", axis=0, tiled=True),
    )
    w_in_back, w_down_back = (
        lax.all_gather(mlp_in, "fsdp", axis=0, tiled=True),
        lax.all_gather(mlp_out, "fsdp", axis=0, tiled=True),
    )
    cot_rows = jnp.dot(select, cotangent, preferred_element_type=jnp.float32)
    grad_rate = jnp.sum(cot_rows * update, axis=-1)
    grad_update = cot_rows * router_rate[:, None]
    grad_expanded = grad_update.astype(jnp.bfloat16)
    grad_down = jnp.einsum("kf,kd->fd", active, grad_expanded, preferred_element_type=jnp.float32)
    grad_active = jnp.einsum(
        "kd,fd->kf", grad_expanded, w_down_back, preferred_element_type=jnp.float32
    )
    (grad_inner_float,) = gelu_pull(grad_active)
    grad_inner = grad_inner_float.astype(jnp.bfloat16)
    grad_up = jnp.einsum("kd,kf->df", normed_two, grad_inner, preferred_element_type=jnp.float32)
    grad_normed_two = jnp.einsum(
        "kf,df->kd", grad_inner, w_in_back, preferred_element_type=jnp.float32
    )
    grad_middle, grad_gain_two = middle_pull(grad_normed_two)
    grad_attended = (grad_update + grad_middle).astype(jnp.bfloat16)
    grad_proj = jnp.einsum("ka,kd->ad", attn_mix, grad_attended, preferred_element_type=jnp.float32)
    grad_mix = jnp.einsum(
        "kd,ad->ka", grad_attended, w_out_back, preferred_element_type=jnp.float32
    ).astype(jnp.bfloat16)
    grad_mix_heads = split_heads(grad_mix)
    scores_again = masked_scores(query_heads, key_heads, allowed, score_scale)
    prob_float = jnp.where(allowed[None], jnp.exp(scores_again - log_total), 0.0)
    grad_probs = jnp.einsum(
        "qhd,khd->hqk", grad_mix_heads, value_heads, preferred_element_type=jnp.float32
    )
    row_delta = jnp.sum(prob_float * grad_probs, axis=-1, keepdims=True)
    grad_scores = (prob_float * (grad_probs - row_delta)).astype(jnp.bfloat16)
    prob_low = prob_float.astype(jnp.bfloat16)
    grad_query = (
        jnp.einsum("hqk,khd->qhd", grad_scores, key_heads, preferred_element_type=jnp.float32)
        * score_scale
    )
    grad_key = (
        jnp.einsum("hqk,qhd->khd", grad_scores, query_heads, preferred_element_type=jnp.float32)
        * score_scale
    )
    grad_value = jnp.einsum(
        "hqk,qhd->khd", prob_low, grad_mix_heads, preferred_element_type=jnp.float32
    )
    grad_qkv = jnp.concatenate(
        [
            grad_query.reshape(row_count, model_width),
            grad_key.reshape(row_count, model_width),
            grad_value.reshape(row_count, model_width),
        ],
        axis=1,
    ).astype(jnp.bfloat16)
    grad_proj_in = jnp.einsum("kd,ke->de", normed, grad_qkv, preferred_element_type=jnp.float32)
    grad_normed = jnp.einsum("ke,de->kd", grad_qkv, w_qkv_back, preferred_element_type=jnp.float32)
    grad_routed_norm, grad_gain_one = norm_pull(grad_normed)
    grad_routed = (
        grad_routed_norm + grad_middle + grad_rate[:, None] * router.astype(jnp.float32)
    ).astype(jnp.bfloat16)
    grad_tokens = (
        cotangent.astype(jnp.float32)
        + jnp.einsum("kt,kd->td", select, grad_routed, preferred_element_type=jnp.float32)
    ).astype(jnp.bfloat16)
    router_local = jnp.dot(grad_rate, routed, precision=lax.Precision.HIGHEST)
    shard_up, shard_down, shard_gain_two = (
        lax.psum_scatter(grad_up, "fsdp", scatter_dimension=0, tiled=True),
        lax.psum_scatter(grad_down, "fsdp", scatter_dimension=0, tiled=True),
        lax.psum_scatter(grad_gain_two, "fsdp", scatter_dimension=0, tiled=True),
    )
    shard_qkv, shard_proj, shard_gain_one = (
        lax.psum_scatter(grad_proj_in, "fsdp", scatter_dimension=0, tiled=True),
        lax.psum_scatter(grad_proj, "fsdp", scatter_dimension=0, tiled=True),
        lax.psum_scatter(grad_gain_one, "fsdp", scatter_dimension=0, tiled=True),
    )
    summed = (
        lax.psum(shard_qkv.astype(jnp.bfloat16), "dp").astype(jnp.float32),
        lax.psum(shard_proj.astype(jnp.bfloat16), "dp").astype(jnp.float32),
        lax.psum(shard_up.astype(jnp.bfloat16), "dp").astype(jnp.float32),
        lax.psum(shard_down.astype(jnp.bfloat16), "dp").astype(jnp.float32),
        lax.psum(shard_gain_one.astype(jnp.bfloat16), "dp").astype(jnp.float32),
        lax.psum(shard_gain_two.astype(jnp.bfloat16), "dp").astype(jnp.float32),
    )
    grad_router = lax.psum(router_local, ("fsdp", "dp"))
    return (
        output,
        grad_tokens,
        summed[0],
        summed[1],
        summed[2],
        summed[3],
        summed[4],
        summed[5],
        grad_router,
    )


def solution(mesh):
    placed = (
        P(("fsdp", "dp"), None),
        P(("fsdp", "dp"), None),
        P(("fsdp", "dp")),
        P(("fsdp", "dp")),
        P("fsdp", None),
        P("fsdp", None),
        P("fsdp", None),
        P("fsdp", None),
        P("fsdp"),
        P("fsdp"),
        P(),
    )
    return jax.shard_map(
        per_device,
        mesh=mesh,
        in_specs=placed,
        out_specs=(
            P(("fsdp", "dp"), None),
            P(("fsdp", "dp"), None),
            P("fsdp", None),
            P("fsdp", None),
            P("fsdp", None),
            P("fsdp", None),
            P("fsdp"),
            P("fsdp"),
            P(),
        ),
        check_vma=False,
    )
```

profile of v0, /device:TPU:0, one launch (start us, length us, event | category | flops | bytes accessed | tf_op | source)
XLA Modules:
  0.0 773.5 jit_solution(13917479941379814595)
XLA Ops:
  10.0 10.4 %all-gather = bf16[8,1,128]{2,1,0:T(2,128)(2,1)S(1)} all-gather(bf16[1,1,128]{2,1,0:T(2,128)(2,1)} %bitcast.84), channel_id=1, replica_groups=mesh['fsdp'=8,'dp'=4] {'fsdp'}, dimensions={0}, use_global_device_ids=true | all-gather | bytes 2304 | tf_op jit(solution)/shard_map/all_gather | solution.py:53
  40.1 9.3 %fusion.12 = f32[512,1024]{1,0:T(8,128)} fusion(bf16[4096,1024]{1,0:T(8,128)(2,1)} %param.12, s32[512]{0:T(512)S(1)} %copy-done.10), kind=kOutput, calls=%fused_computation.24 | convolution fusion | flops 4297064448 | bytes 10487808 | tf_op jit(solution)/shard_map/dot_general | solution.py:106
  72.4 9.1 %fusion.1 = (f32[16,512]{1,0:T(8,128)S(1)}, f32[16,512,512]{1,2,0:T(8,128)}) fusion(pred[512,512]{0,1:T(8,128)(4,1)S(1)} %compare_and_fusion, bf16[512,16,64]{0,2,1:T(8,128)(2,1)} %bitcast.57, bf16[512,16,64]{0,2,1:T(8,128)(2,1)S(1)} %bitcast.55), kind=kOutput, calls=%fused_computation.11 | convolution fusion | flops 549445632 | bytes 19169280 | tf_op jit(solution)/shard_map/qhd,khd->hqk/dot_general | solution.py:28
  81.5 9.3 %fusion = f32[16,512]{1,0:T(8,128)S(1)} fusion(f32[16,512,512]{1,2,0:T(8,128)} %get-tuple-element.31, f32[16,512]{1,0:T(8,128)S(1)} %get-tuple-element.30, pred[512,512]{0,1:T(8,128)(4,1)S(1)} %compare_and_fusion), kind=kLoop, calls=%fused_computation.8 | loop fusion | flops 16769024 | bytes 17104896 | tf_op jit(solution)/shard_map/reduce_sum | solution.py:77
  90.8 9.6 %fusion.23 = bf16[16,64,512]{2,1,0:T(8,128)(2,1)} fusion(bf16[512,16,64]{0,2,1:T(8,128)(2,1)} %bitcast.65, f32[16,512,512]{1,2,0:T(8,128)} %get-tuple-element.31, f32[16,512]{1,0:T(8,128)S(1)} %fusion, f32[16,512]{1,0:T(8,128)S(1)} %get-tuple-element.30, pred[512,512]{0,1:T(8,128)(4,1)S(1)} %compare_and_fusion), kind=kOutput, calls=%fused_computation.54 | convolution fusion | flops 558366720 | bytes 19202048 | tf_op jit(solution)/shard_map/hqk,khd->qhd/dot_general | solution.py:80
  105.6 38.3 %all-gather.11.cloned.1.call-done = bf16[1024,4096]{1,0:T(8,128)(2,1)} async-done(((bf16[128,4096]{1,0:T(8,128)(2,1)}), bf16[1024,4096]{1,0:T(8,128)(2,1)}) %all-gather.11.cloned.1.call-update) | async-done | bytes 8388624 | tf_op jit(solution)/shard_map/all_gather | solution.py:57
  143.9 12.1 %fusion.50 = f32[512,4096]{1,0:T(8,128)} fusion(bf16[1024,4096]{1,0:T(8,128)(2,1)} %all-gather.11.cloned.1.call-done, f32[512,1024]{1,0:T(8,128)} %get-tuple-element.22, f32[1024]{0:T(1024)S(1)} %bitcast.74, f32[512]{0:T(512)S(1)} %fusion.39), kind=kOutput, calls=%fused_computation.88 | convolution fusion | flops 4296540160 | bytes 18880512 | tf_op jit(solution)/shard_map/dot_general | solution.py:88
  156.0 44.0 %all-gather.13.cloned.1.call-done = bf16[4096,1024]{1,0:T(8,128)(2,1)} async-done(((bf16[512,1024]{1,0:T(8,128)(2,1)}), bf16[4096,1024]{1,0:T(8,128)(2,1)}) %all-gather.13.cloned.1.call-update) | async-done | bytes 8388624 | tf_op jit(solution)/shard_map/all_gather | solution.py:58
  200.0 14.6 %fusion.8 = bf16[512,4096]{1,0:T(8,128)(2,1)} fusion(f32[512,4096]{1,0:T(8,128)} %fusion.50, bf16[4096,1024]{1,0:T(8,128)(2,1)} %all-gather.13.cloned.1.call-done, f32[512,1024]{1,0:T(8,128)} %fusion.12, f32[512]{0:T(512)S(1)} %bitcast.79), kind=kOutput, calls=%fused_computation.18 | convolution fusion | flops 4337958912 | bytes 23070720 | tf_op jit(solution)/shard_map/kd,fd->kf/dot_general | solution.py:111
  214.6 10.9 %multiply_reduce_fusion.1 = (f32[1024]{0:T(1024)S(1)}, f32[512]{0:T(512)S(1)}, f32[512,1024]{1,0:T(8,128)}) fusion(f32[512,1024]{1,0:T(8,128)S(1)} %copy-done.1, f32[512]{0:T(512)S(1)} %fusion.39, f32[1024]{0:T(1024)S(1)} %bitcast.75, bf16[512,4096]{1,0:T(8,128)(2,1)} %fusion.8, bf16[1024,4096]{1,0:T(8,128)(2,1)} %all-gather.11.cloned.1.call-done), kind=kOutput, calls=%fused_computation.39 | convolution fusion | flops 4298111488 | bytes 16789504 | tf_op jit(solution)/shard_map/kf,df->kd/dot_general | solution.py:117
  225.5 10.1 %multiply_reduce_fusion.3 = (f32[512]{0:T(512)S(1)}, bf16[512,1024]{1,0:T(8,128)(2,1)S(1)}, f32[512,1024]{1,0:T(8,128)}) fusion(f32[512,1024]{1,0:T(8,128)S(1)} %copy-done.19, f32[512,1024]{1,0:T(8,128)S(1)} %copy-done.1, f32[512]{0:T(512)S(1)} %multiply_multiply_fusion.3, f32[512]{0:T(512)S(1)} %fusion.39, f32[512,1024]{1,0:T(8,128)} %get-tuple-element.33, ...), kind=kOutput, calls=%fused_computation.41 | convolution fusion | flops 4319608320 | bytes 28323840 | tf_op jit(solution)/shard_map/dot_general | solution.py:91
  246.4 13.6 %multiply_reduce_fusion = (f32[16,512]{1,0:T(8,128)S(1)}, f32[16,512,512]{1,2,0:T(8,128)}) fusion(f32[16,512]{1,0:T(8,128)S(1)} %log_add_fusion, f32[16,512,512]{1,2,0:T(8,128)} %get-tuple-element.31, pred[512,512]{0,1:T(8,128)(4,1)S(1)} %compare_and_fusion, bf16[512,16,64]{0,2,1:T(8,128)(2,1)} %bitcast.67, bf16[512,16,64]{0,2,1:T(8,128)(2,1)} %bitcast.66), kind=kOutput, calls=%fused_computation.2 | convolution fusion | flops 562028544 | bytes 35979264 | tf_op jit(solution)/shard_map/qhd,khd->hqk/dot_general | solution.py:129
  259.9 13.2 %multiply_convert_fusion = bf16[16,512,512]{1,2,0:T(8,128)(2,1)S(1)} fusion(f32[16,512,512]{1,2,0:T(8,128)} %get-tuple-element.36, f32[16,512]{1,0:T(8,128)S(1)} %get-tuple-element.35, f32[16,512]{1,0:T(8,128)S(1)} %log_add_fusion, f32[16,512,512]{1,2,0:T(8,128)} %get-tuple-element.31, pred[512,512]{0,1:T(8,128)(4,1)S(1)} %compare_and_fusion), kind=kLoop, calls=%fused_computation.1 | loop fusion | flops 29360128 | bytes 42270720 | tf_op jit(solution)/shard_map/convert_element_type | solution.py:133
  287.0 9.9 %fusion.27 = f32[1024,3072]{1,0:T(8,128)} fusion(bf16[512,1024]{0,1:T(8,128)(2,1)S(1)} %bitcast.88, bf16[512,1024]{0,1:T(8,128)(2,1)S(1)} %bitcast.63, bf16[512,1024]{0,1:T(8,128)(2,1)S(1)} %bitcast.59, f32[512,1024]{1,0:T(8,128)S(1)} %get-tuple-element.29, f32[1024]{0:T(1024)S(1)} %bitcast.71, f32[512]{0:T(512)S(1)} %fusion.38), kind=kOutput, calls=%fused_computation.57 | convolution fusion | flops 3232235520 | bytes 17831936 | tf_op jit(solution)/shard_map/kd,ke->de/dot_general | solution.py:154
  296.9 19.0 %fusion.47 = f32[4096,1024]{1,0:T(8,128)} fusion(f32[512,1024]{1,0:T(8,128)} %fusion.12, f32[512]{0:T(512)S(1)} %bitcast.81, f32[512,4096]{1,0:T(8,128)} %fusion.50), kind=kOutput, calls=%fused_computation.85 | convolution fusion | flops 4314890240 | bytes 27265024 | tf_op jit(solution)/shard_map/kf,kd->fd/dot_general | solution.py:110
  316.2 15.3 %fusion.49 = f32[1024,4096]{1,0:T(8,128)} fusion(bf16[512,4096]{1,0:T(8,128)(2,1)} %fusion.8, f32[512,1024]{1,0:T(8,128)} %get-tuple-element.22, f32[1024]{0:T(1024)S(1)} %bitcast.77, f32[512]{0:T(512)S(1)} %fusion.39), kind=kOutput, calls=%fused_computation.87 | convolution fusion | flops 4296540160 | bytes 23074816 | tf_op jit(solution)/shard_map/kd,kf->df/dot_general | solution.py:116
  341.9 15.5 %all-reduce.2 = (bf16[1024]{0:T(1024)(128)(2,1)S(1)}, bf16[1024]{0:T(1024)(128)(2,1)S(1)}) all-reduce(f32[1024]{0:T(1024)S(1)} %get-tuple-element.11, f32[1024]{0:T(1024)S(1)} %get-tuple-element.9), channel_id=6, replica_groups=mesh['fsdp'=8,'dp'=4] {'fsdp'}, use_global_device_ids=true, to_apply=%region_19.20.clone | all-reduce | flops 2048 | bytes 12288
  357.6 11.7 %all-reduce.3 = (bf16[128]{0:T(256)(128)(2,1)S(1)}, bf16[128]{0:T(256)(128)(2,1)S(1)}) all-reduce(bf16[128]{0:T(256)(128)(2,1)S(1)} %dynamic-slice.7, bf16[128]{0:T(256)(128)(2,1)S(1)} %dynamic-slice.6), channel_id=1, replica_groups=mesh['fsdp'=8,'dp'=4] {'dp'}, use_global_device_ids=true, to_apply=%region_20.21 | all-reduce | flops 256 | bytes 1024 | tf_op jit(solution)/shard_map/psum | solution.py:180
  371.4 37.7 %psum.55 = f32[1024]{0:T(1024)} all-reduce(f32[1024]{0:T(1024)S(1)} %bitcast.69), channel_id=1, replica_groups=mesh['fsdp'=8,'dp'=4] {'fsdp','dp'}, use_global_device_ids=true, to_apply=%region_24.25 | all-reduce | flops 1024 | bytes 8192 | tf_op jit(solution)/shard_map/psum | solution.py:183
  413.7 100.4 %reduce-scatter.11.cloned.1.call-done = f32[512,1024]{1,0:T(8,128)} async-done(((f32[4096,1024]{1,0:T(8,128)}), f32[512,1024]{1,0:T(8,128)}) %reduce-scatter.11.cloned.1.call-update) | async-done | bytes 2097168 | tf_op jit(solution)/shard_map/reduce_scatter | solution.py:167
  516.8 117.0 %reduce-scatter.9.cloned.1.call-done = f32[128,4096]{1,0:T(8,128)} async-done(((f32[1024,4096]{1,0:T(8,128)}), f32[128,4096]{1,0:T(8,128)}) %reduce-scatter.9.cloned.1.call-update) | async-done | bytes 2097168 | tf_op jit(solution)/shard_map/reduce_scatter | solution.py:166
  636.6 10.0 %add_convert_fusion.1 = bf16[4096,1024]{1,0:T(8,128)(2,1)} fusion(bf16[4096,1024]{1,0:T(8,128)(2,1)} %param.11, s32[512]{0:T(512)S(1)} %copy-done.11, f32[512,1024]{1,0:T(8,128)} %get-tuple-element.34, f32[512]{0:T(512)S(1)} %bitcast.82), kind=kOutput, calls=%fused_computation.4 | convolution fusion | flops 4310695936 | bytes 18878464 | tf_op jit(solution)/shard_map/kt,kd->td/dot_general | solution.py:96
  646.6 11.4 %add_convert_fusion = bf16[4096,1024]{1,0:T(8,128)(2,1)} fusion(bf16[4096,1024]{1,0:T(8,128)(2,1)} %param.12, s32[512]{0:T(512)S(1)} %copy-done.11, f32[512,1024]{1,0:T(8,128)S(1)} %get-tuple-element.29, f32[512,1024]{1,0:T(8,128)S(1)} %copy-done.20, f32[1024]{0:T(1024)S(1)} %convert_element_type.135, f32[512]{0:T(512)S(1)} %get-tuple-element.26, ...), kind=kOutput, calls=%fused_computation | convolution fusion | flops 4316987392 | bytes 25190400 | tf_op jit(solution)/shard_map/kt,kd->td/dot_general | solution.py:162
  658.0 100.1 %all-reduce.7.cloned.1.call-done = (bf16[128,3072]{1,0:T(8,128)(2,1)}, bf16[128,1024]{1,0:T(8,128)(2,1)}, bf16[128,4096]{1,0:T(8,128)(2,1)}, bf16[512,1024]{1,0:T(8,128)(2,1)}) async-done(((bf16[128,3072]{1,0:T(8,128)(2,1)}, bf16[128,1024]{1,0:T(8,128)(2,1)}, bf16[128,4096]{1,0:T(8,128)(2,1)}, bf16[512,1024]{1,0:T(8,128)(2,1)}), (bf16[128,3072]{1,0:T(8,128)(2,1)}, bf16[128,1024]{1,0:T(8,128)(2,1)}, ...) | async-done | bytes 3145744 | tf_op jit(solution)/shard_map/psum | solution.py:176
  (108 shorter events, 106.1 us)
Async XLA Ops:
  7.2 50.9 %all-gather.7.cloned.1.call-start = ((), (), s32[]{:S(2)}) async-start(), calls=%async_computation.4 | async-start | bytes 7077888 | tf_op jit(solution)/shard_map/all_gather | solution.py:51
  7.9 92.5 %all-gather.9.cloned.1.call-start = ((), (), s32[]{:S(2)}) async-start(), calls=%async_computation.5 | async-start | bytes 2359296 | tf_op jit(solution)/shard_map/all_gather | solution.py:52
  8.7 135.3 %all-gather.11.cloned.1.call-start = ((), (), s32[]{:S(2)}) async-start(), calls=%async_computation.6 | async-start | bytes 9437184 | tf_op jit(solution)/shard_map/all_gather | solution.py:57
  9.4 190.6 %all-gather.13.cloned.1.call-start = ((), (), s32[]{:S(2)}) async-start(), calls=%async_computation.7 | async-start | bytes 9437184 | tf_op jit(solution)/shard_map/all_gather | solution.py:58
  10.0 399.2 %reduce-scatter.7.cloned.1.call-start = ((), (), s32[]{:S(2)}) async-start(), calls=%async_computation.9 | async-start | bytes 4718592 | tf_op jit(solution)/shard_map/reduce_scatter | solution.py:172
  31.6 7.8 %copy-start.10 = (s32[512]{0:T(512)S(1)}, s32[512]{0:T(512)}, u32[]{:S(2)}) copy-start(s32[512]{0:T(512)} %param.14) | copy-start | bytes 6148
  200.0 14.6 %copy-start.1 = (f32[512,1024]{1,0:T(8,128)S(1)}, f32[512,1024]{1,0:T(8,128)}, u32[]{:S(2)}) copy-start(f32[512,1024]{1,0:T(8,128)} %get-tuple-element.22) | copy-start | bytes 6291460
  214.6 10.9 %copy-start.3 = (f32[512,1024]{1,0:T(8,128)S(1)}, f32[512,1024]{1,0:T(8,128)}, u32[]{:S(2)}) copy-start(f32[512,1024]{1,0:T(8,128)} %get-tuple-element.32) | copy-start | bytes 6291460
  214.6 10.9 %copy-start.15 = (bf16[4096,1024]{1,0:T(8,128)(2,1)S(1)}, bf16[4096,1024]{1,0:T(8,128)(2,1)}, u32[]{:S(2)}) copy-start(bf16[4096,1024]{1,0:T(8,128)(2,1)} %all-gather.13.cloned.1.call-done) | copy-start | bytes 25165828
  214.6 10.9 %copy-start.19 = (f32[512,1024]{1,0:T(8,128)S(1)}, f32[512,1024]{1,0:T(8,128)}, u32[]{:S(2)}) copy-start(f32[512,1024]{1,0:T(8,128)} %fusion.12) | copy-start | bytes 6291460
  225.5 11.1 %copy-start.6 = (bf16[16,64,512]{2,1,0:T(8,128)(2,1)S(1)}, bf16[16,64,512]{2,1,0:T(8,128)(2,1)}, u32[]{:S(2)}) copy-start(bf16[16,64,512]{2,1,0:T(8,128)(2,1)} %fusion.23) | copy-start | bytes 3145732
  246.3 164.7 %reduce-scatter.5.cloned.1.call-start = ((), (), s32[]{:S(2)}) async-start(), calls=%async_computation.8 | async-start | bytes 14155776 | tf_op jit(solution)/shard_map/reduce_scatter | solution.py:171
  259.9 13.2 %copy-start = (bf16[512,1024]{0,1:T(8,128)(2,1)S(1)}, bf16[512,1024]{0,1:T(8,128)(2,1)}, u32[]{:S(2)}) copy-start(bf16[512,1024]{0,1:T(8,128)(2,1)} %copy.49) | copy-start | bytes 3145732
  275.7 10.3 %copy-start.7 = (bf16[16,64,512]{2,1,0:T(8,128)(2,1)}, bf16[16,64,512]{2,1,0:T(8,128)(2,1)S(1)}, u32[]{:S(2)}) copy-start(bf16[16,64,512]{2,1,0:T(8,128)(2,1)S(1)} %multiply_convert_fusion.2) | copy-start | bytes 3145732
  277.4 8.7 %copy-start.4 = (bf16[16,64,512]{2,1,0:T(8,128)(2,1)}, bf16[16,64,512]{2,1,0:T(8,128)(2,1)S(1)}, u32[]{:S(2)}) copy-start(bf16[16,64,512]{2,1,0:T(8,128)(2,1)S(1)} %multiply_convert_fusion.3) | copy-start | bytes 3145732
  296.9 217.2 %reduce-scatter.11.cloned.1.call-start = ((), (), s32[]{:S(2)}) async-start(), calls=%async_computation.11 | async-start | bytes 18874368 | tf_op jit(solution)/shard_map/reduce_scatter | solution.py:167
  316.0 317.8 %reduce-scatter.9.cloned.1.call-start = ((), (), s32[]{:S(2)}) async-start(), calls=%async_computation.10 | async-start | bytes 18874368 | tf_op jit(solution)/shard_map/reduce_scatter | solution.py:166
  331.6 426.6 %all-reduce.7.cloned.1.call-start = ((), (), s32[]{:S(2)}) async-start(), calls=%async_computation.12 | async-start | bytes 6291456 | tf_op jit(solution)/shard_map/psum | solution.py:176
  333.5 75.7 %copy-start.14 = (f32[512]{0:T(512)S(1)}, f32[512]{0:T(512)}, u32[]{:S(2)}) copy-start(f32[512]{0:T(512)} %copy-done.13) | copy-start | bytes 6148
  409.2 227.4 %copy-start.11 = (s32[512]{0:T(512)S(1)}, s32[512]{0:T(512)}, u32[]{:S(2)}) copy-start(s32[512]{0:T(512)} %param.14) | copy-start | bytes 6148
  636.5 10.1 %copy-start.2 = (f32[512,1024]{1,0:T(8,128)S(1)}, f32[512,1024]{1,0:T(8,128)}, u32[]{:S(2)}) copy-start(f32[512,1024]{1,0:T(8,128)} %get-tuple-element.22) | copy-start | bytes 6291460
  636.6 10.1 %copy-start.20 = (f32[512,1024]{1,0:T(8,128)S(1)}, f32[512,1024]{1,0:T(8,128)}, u32[]{:S(2)}) copy-start(f32[512,1024]{1,0:T(8,128)} %get-tuple-element.37) | copy-start | bytes 6291460
  636.6 10.0 %copy-start.21 = (f32[512,1024]{1,0:T(8,128)S(1)}, f32[512,1024]{1,0:T(8,128)}, u32[]{:S(2)}) copy-start(f32[512,1024]{1,0:T(8,128)} %get-tuple-element.33) | copy-start | bytes 6291460
  758.1 7.1 copy-start.8
  (7 other events, 7.6 us)
Sparse Core Ops, SparseCore 0:
  9.9 48.1 all-gather.6
  59.9 27.7 all-gather.8
  89.6 54.2 all-gather.10
  145.7 54.2 all-gather.12
  246.4 51.1 reduce-scatter.6
  301.0 93.5 reduce-scatter.4
  398.2 115.8 reduce-scatter.10
  517.6 116.1 reduce-scatter.8
  637.0 121.0 all-reduce.6
where the time goes:
time: 783 us; the launch traced here: 774 us
  waiting for transfers between devices  411 us (52%)
  matrix products  204 us (26%)
  blocking collectives  84.2 us (11%)
  other arithmetic  44 us (6%)
  between operations  15 us (2%)
  local copies, waits for them, and re-layouts  14.3 us (2%)
    reduce_scatter x1, waiting for transfers between devices, per_device(): lax.psum_scatter(grad_up, 'fsdp', scatter_dimension=0, tiled=True)  117 us
    reduce_scatter x1, waiting for transfers between devices, per_device(): lax.psum_scatter(grad_down, 'fsdp', scatter_dimension=0, tiled=True)  100 us
    psum x1, waiting for transfers between devices, per_device(): lax.psum(shard_qkv.astype(jnp.bfloat16), 'dp').astype(jnp.float32)  100 us
    all_gather x1, waiting for transfers between devices, per_device(): lax.all_gather(mlp_out, 'fsdp', axis=0, tiled=True)  44 us
    all_gather x1, waiting for transfers between devices, per_device(): lax.all_gather(mlp_in, 'fsdp', axis=0, tiled=True)  38.3 us
    psum x1, blocking collectives, per_device(): grad_router = lax.psum(router_local, ('fsdp', 'dp'))  37.7 us
    dot_general x1, matrix products, per_device(): jnp.einsum('kf,kd->fd', active, grad_expanded, preferred_element_type=jnp...  19 us
  transfers between devices with their start and end apart: 9, of which 6 were waited for; matrix products, arithmetic and copies ran while one was open for 26% of the time, Pallas kernels for 0%

commit v1 on v0

--- a/solution.py
+++ b/solution.py
@@ -173,7 +173,7 @@
         lax.psum_scatter(grad_gain_one, "fsdp", scatter_dimension=0, tiled=True),
     )
     summed = (
-        lax.psum(shard_qkv.astype(jnp.bfloat16), "dp").astype(jnp.float32),
+        jnp.sum(lax.all_gather(shard_qkv.astype(jnp.bfloat16), "dp"), axis=0).astype(jnp.float32),
         lax.psum(shard_proj.astype(jnp.bfloat16), "dp").astype(jnp.float32),
         lax.psum(shard_up.astype(jnp.bfloat16), "dp").astype(jnp.float32),
         lax.psum(shard_down.astype(jnp.bfloat16), "dp").astype(jnp.float32),

time: 783 us -> 864 us (1.10)
  waiting for transfers between devices: 411 us -> 489 us
    reduce_scatter x1, waiting for transfers between devices: 0.01 us -> 55.1 us  [per_device(): lax.psum_scatter(grad_proj_in, 'fsdp', scatter_dimension=0, tiled=True)]
    reduce_scatter x1, waiting for transfers between devices: 100 us -> 118 us  [per_device(): lax.psum_scatter(grad_down, 'fsdp', scatter_dimension=0, tiled=True)]
  transfers between devices with their start and end apart: 9 -> 10, of which waited for: 6 -> 9; matrix products, arithmetic and copies ran while one was open for 26% -> 19% of each run, Pallas kernels for 0% -> 0%
where the time goes in v1:
time: 864 us; the launch traced here: 855 us
  waiting for transfers between devices  489 us (57%)
  matrix products  203 us (23%)
  blocking collectives  86.7 us (10%)
  other arithmetic  45.5 us (5%)
  between operations  15.4 us (2%)
  local copies, waits for them, and re-layouts  14.7 us (2%)
    reduce_scatter x1, waiting for transfers between devices, per_device(): lax.psum_scatter(grad_down, 'fsdp', scatter_dimension=0, tiled=True)  118 us
    reduce_scatter x1, waiting for transfers between devices, per_device(): lax.psum_scatter(grad_up, 'fsdp', scatter_dimension=0, tiled=True)  117 us
    psum x1, waiting for transfers between devices, per_device(): lax.psum(shard_proj.astype(jnp.bfloat16), 'dp').astype(jnp.float32)  92.6 us
    reduce_scatter x1, waiting for transfers between devices, per_device(): lax.psum_scatter(grad_proj_in, 'fsdp', scatter_dimension=0, tiled=True)  55.1 us
    all_gather x1, waiting for transfers between devices, per_device(): lax.all_gather(mlp_out, 'fsdp', axis=0, tiled=True)  44 us
    psum x1, blocking collectives, per_device(): grad_router = lax.psum(router_local, ('fsdp', 'dp'))  42.8 us
    all_gather x1, waiting for transfers between devices, per_device(): lax.all_gather(mlp_in, 'fsdp', axis=0, tiled=True)  38.3 us
    dot_general x1, matrix products, per_device(): jnp.einsum('kf,kd->fd', active, grad_expanded, preferred_element_type=jnp...  17.8 us
  transfers between devices with their start and end apart: 10, of which 9 were waited for; matrix products, arithmetic and copies ran while one was open for 19% of the time, Pallas kernels for 0%

profile of v1, /device:TPU:0, one launch (start us, length us, event | category | flops | bytes accessed | tf_op | source)
XLA Modules:
  0.0 855.1 jit_solution(15725409342789099442)
XLA Ops:
  10.0 10.4 %all-gather.1 = bf16[8,1,128]{2,1,0:T(2,128)(2,1)S(1)} all-gather(bf16[1,1,128]{2,1,0:T(2,128)(2,1)} %bitcast.86), channel_id=1, replica_groups=mesh['fsdp'=8,'dp'=4] {'fsdp'}, dimensions={0}, use_global_device_ids=true | all-gather | bytes 2304 | tf_op jit(solution)/shard_map/all_gather | solution.py:53
  81.6 9.3 %fusion = f32[16,512]{1,0:T(8,128)S(1)} fusion(f32[16,512,512]{1,2,0:T(8,128)} %get-tuple-element.30, f32[16,512]{1,0:T(8,128)S(1)} %get-tuple-element.29, pred[512,512]{0,1:T(8,128)(4,1)S(1)} %compare_and_fusion), kind=kLoop, calls=%fused_computation.8 | loop fusion | flops 16769024 | bytes 17104896 | tf_op jit(solution)/shard_map/reduce_sum | solution.py:77
  90.9 9.5 %fusion.23 = bf16[16,64,512]{2,1,0:T(8,128)(2,1)} fusion(bf16[512,16,64]{0,2,1:T(8,128)(2,1)} %bitcast.67, f32[16,512,512]{1,2,0:T(8,128)} %get-tuple-element.30, f32[16,512]{1,0:T(8,128)S(1)} %fusion, f32[16,512]{1,0:T(8,128)S(1)} %get-tuple-element.29, pred[512,512]{0,1:T(8,128)(4,1)S(1)} %compare_and_fusion), kind=kOutput, calls=%fused_computation.54 | convolution fusion | flops 558366720 | bytes 19202048 | tf_op jit(solution)/shard_map/hqk,khd->qhd/dot_general | solution.py:80
  105.6 38.3 %all-gather.13.cloned.1.call-done = bf16[1024,4096]{1,0:T(8,128)(2,1)} async-done(((bf16[128,4096]{1,0:T(8,128)(2,1)}), bf16[1024,4096]{1,0:T(8,128)(2,1)}) %all-gather.13.cloned.1.call-update) | async-done | bytes 8388624 | tf_op jit(solution)/shard_map/all_gather | solution.py:57
  143.9 12.1 %fusion.50 = f32[512,4096]{1,0:T(8,128)} fusion(bf16[1024,4096]{1,0:T(8,128)(2,1)} %all-gather.13.cloned.1.call-done, f32[512,1024]{1,0:T(8,128)} %get-tuple-element.21, f32[1024]{0:T(1024)S(1)} %bitcast.76, f32[512]{0:T(512)S(1)} %fusion.39), kind=kOutput, calls=%fused_computation.88 | convolution fusion | flops 4296540160 | bytes 18880512 | tf_op jit(solution)/shard_map/dot_general | solution.py:88
  156.0 44.0 %all-gather.15.cloned.1.call-done = bf16[4096,1024]{1,0:T(8,128)(2,1)} async-done(((bf16[512,1024]{1,0:T(8,128)(2,1)}), bf16[4096,1024]{1,0:T(8,128)(2,1)}) %all-gather.15.cloned.1.call-update) | async-done | bytes 8388624 | tf_op jit(solution)/shard_map/all_gather | solution.py:58
  200.0 14.6 %fusion.8 = bf16[512,4096]{1,0:T(8,128)(2,1)} fusion(f32[512,4096]{1,0:T(8,128)} %fusion.50, bf16[4096,1024]{1,0:T(8,128)(2,1)} %all-gather.15.cloned.1.call-done, f32[512,1024]{1,0:T(8,128)} %fusion.12, f32[512]{0:T(512)S(1)} %bitcast.81), kind=kOutput, calls=%fused_computation.18 | convolution fusion | flops 4337958912 | bytes 23070720 | tf_op jit(solution)/shard_map/kd,fd->kf/dot_general | solution.py:111
  214.6 10.9 %multiply_reduce_fusion.1 = (f32[1024]{0:T(1024)S(1)}, f32[512]{0:T(512)S(1)}, f32[512,1024]{1,0:T(8,128)}) fusion(f32[512,1024]{1,0:T(8,128)S(1)} %copy-done.1, f32[512]{0:T(512)S(1)} %fusion.39, f32[1024]{0:T(1024)S(1)} %bitcast.77, bf16[512,4096]{1,0:T(8,128)(2,1)} %fusion.8, bf16[1024,4096]{1,0:T(8,128)(2,1)} %all-gather.13.cloned.1.call-done), kind=kOutput, calls=%fused_computation.39 | convolution fusion | flops 4298111488 | bytes 16789504 | tf_op jit(solution)/shard_map/kf,df->kd/dot_general | solution.py:117
  225.5 10.2 %multiply_reduce_fusion.3 = (f32[512]{0:T(512)S(1)}, bf16[512,1024]{1,0:T(8,128)(2,1)S(1)}, f32[512,1024]{1,0:T(8,128)}) fusion(f32[512,1024]{1,0:T(8,128)S(1)} %copy-done.19, f32[512,1024]{1,0:T(8,128)S(1)} %copy-done.1, f32[512]{0:T(512)S(1)} %multiply_multiply_fusion.3, f32[512]{0:T(512)S(1)} %fusion.39, f32[512,1024]{1,0:T(8,128)} %get-tuple-element.32, ...), kind=kOutput, calls=%fused_computation.41 | convolution fusion | flops 4319608320 | bytes 28323840 | tf_op jit(solution)/shard_map/dot_general | solution.py:91
  241.2 10.6 %fusion.24 = bf16[16,64,512]{2,1,0:T(8,128)(2,1)S(1)} fusion(bf16[512,16,64]{0,2,1:T(8,128)(2,1)} %bitcast.69, f32[16,512]{1,0:T(8,128)S(1)} %log_add_fusion, f32[16,512,512]{1,2,0:T(8,128)} %get-tuple-element.30, pred[512,512]{0,1:T(8,128)(4,1)S(1)} %compare_and_fusion), kind=kOutput, calls=%fused_computation.56 | convolution fusion | flops 558366720 | bytes 19169280 | tf_op jit(solution)/shard_map/hqk,qhd->khd/dot_general | solution.py:143
  251.8 12.8 %multiply_reduce_fusion = (f32[16,512]{1,0:T(8,128)S(1)}, f32[16,512,512]{1,2,0:T(8,128)}) fusion(f32[16,512]{1,0:T(8,128)S(1)} %log_add_fusion, f32[16,512,512]{1,2,0:T(8,128)} %get-tuple-element.30, pred[512,512]{0,1:T(8,128)(4,1)S(1)} %compare_and_fusion, bf16[512,16,64]{0,2,1:T(8,128)(2,1)S(1)} %bitcast.70, bf16[512,16,64]{0,2,1:T(8,128)(2,1)S(1)} %bitcast.68), kind=kOutput, calls=%fused_computation.2 | convolution fusion | flops 562028544 | bytes 35979264 | tf_op jit(solution)/shard_map/qhd,khd->hqk/dot_general | solution.py:129
  264.6 12.4 %multiply_convert_fusion = bf16[16,512,512]{1,2,0:T(8,128)(2,1)S(1)} fusion(f32[16,512,512]{1,2,0:T(8,128)} %get-tuple-element.35, f32[16,512]{1,0:T(8,128)S(1)} %get-tuple-element.34, f32[16,512]{1,0:T(8,128)S(1)} %log_add_fusion, f32[16,512,512]{1,2,0:T(8,128)} %get-tuple-element.30, pred[512,512]{0,1:T(8,128)(4,1)S(1)} %compare_and_fusion), kind=kLoop, calls=%fused_computation.1 | loop fusion | flops 29360128 | bytes 42270720 | tf_op jit(solution)/shard_map/convert_element_type | solution.py:133
  282.2 9.8 %fusion.27 = f32[1024,3072]{1,0:T(8,128)} fusion(bf16[512,1024]{0,1:T(8,128)(2,1)S(1)} %bitcast.90, bf16[512,1024]{0,1:T(8,128)(2,1)S(1)} %bitcast.65, bf16[512,1024]{0,1:T(8,128)(2,1)S(1)} %bitcast.60, f32[512,1024]{1,0:T(8,128)S(1)} %get-tuple-element.28, f32[1024]{0:T(1024)S(1)} %bitcast.73, f32[512]{0:T(512)S(1)} %fusion.38), kind=kOutput, calls=%fused_computation.57 | convolution fusion | flops 3232235520 | bytes 17831936 | tf_op jit(solution)/shard_map/kd,ke->de/dot_general | solution.py:154
  297.7 17.8 %fusion.47 = f32[4096,1024]{1,0:T(8,128)} fusion(f32[512,1024]{1,0:T(8,128)} %fusion.12, f32[512]{0:T(512)S(1)} %bitcast.83, f32[512,4096]{1,0:T(8,128)} %fusion.50), kind=kOutput, calls=%fused_computation.85 | convolution fusion | flops 4314890240 | bytes 27265024 | tf_op jit(solution)/shard_map/kf,kd->fd/dot_general | solution.py:110
  315.8 13.4 %fusion.49 = f32[1024,4096]{1,0:T(8,128)} fusion(bf16[512,4096]{1,0:T(8,128)(2,1)} %fusion.8, f32[512,1024]{1,0:T(8,128)} %get-tuple-element.21, f32[1024]{0:T(1024)S(1)} %bitcast.79, f32[512]{0:T(512)S(1)} %fusion.39), kind=kOutput, calls=%fused_computation.87 | convolution fusion | flops 4296540160 | bytes 23074816 | tf_op jit(solution)/shard_map/kd,kf->df/dot_general | solution.py:116
  329.3 55.1 %reduce-scatter.5.cloned.1.call-done = f32[128,3072]{1,0:T(8,128)} async-done(((f32[1024,3072]{1,0:T(8,128)}), f32[128,3072]{1,0:T(8,128)}) %reduce-scatter.5.cloned.1.call-update) | async-done | bytes 1572880 | tf_op jit(solution)/shard_map/reduce_scatter | solution.py:171
  396.6 12.7 %all-reduce.2 = (bf16[1024]{0:T(1024)(128)(2,1)S(1)}, bf16[1024]{0:T(1024)(128)(2,1)S(1)}) all-reduce(f32[1024]{0:T(1024)S(1)} %get-tuple-element.11, f32[1024]{0:T(1024)S(1)} %get-tuple-element.9), channel_id=7, replica_groups=mesh['fsdp'=8,'dp'=4] {'fsdp'}, use_global_device_ids=true, to_apply=%region_19.20.clone | all-reduce | flops 2048 | bytes 12288
  409.5 11.9 %all-reduce.3 = (bf16[128]{0:T(256)(128)(2,1)S(1)}, bf16[128]{0:T(256)(128)(2,1)S(1)}) all-reduce(bf16[128]{0:T(256)(128)(2,1)S(1)} %dynamic-slice.7, bf16[128]{0:T(256)(128)(2,1)S(1)} %dynamic-slice.6), channel_id=1, replica_groups=mesh['fsdp'=8,'dp'=4] {'dp'}, use_global_device_ids=true, to_apply=%region_20.21 | all-reduce | flops 256 | bytes 1024 | tf_op jit(solution)/shard_map/psum | solution.py:180
  422.4 10.0 %add_convert_fusion.1 = bf16[4096,1024]{1,0:T(8,128)(2,1)} fusion(bf16[4096,1024]{1,0:T(8,128)(2,1)} %param.11, s32[512]{0:T(512)S(1)} %copy-done.11, f32[512,1024]{1,0:T(8,128)} %get-tuple-element.33, f32[512]{0:T(512)S(1)} %bitcast.84), kind=kOutput, calls=%fused_computation.4 | convolution fusion | flops 4310695936 | bytes 18878464 | tf_op jit(solution)/shard_map/kt,kd->td/dot_general | solution.py:96
  440.6 118.0 %reduce-scatter.11.cloned.1.call-done = f32[512,1024]{1,0:T(8,128)} async-done(((f32[4096,1024]{1,0:T(8,128)}), f32[512,1024]{1,0:T(8,128)}) %reduce-scatter.11.cloned.1.call-update) | async-done | bytes 2097168 | tf_op jit(solution)/shard_map/reduce_scatter | solution.py:167
  561.3 117.0 %reduce-scatter.9.cloned.1.call-done = f32[128,4096]{1,0:T(8,128)} async-done(((f32[1024,4096]{1,0:T(8,128)}), f32[128,4096]{1,0:T(8,128)}) %reduce-scatter.9.cloned.1.call-update) | async-done | bytes 2097168 | tf_op jit(solution)/shard_map/reduce_scatter | solution.py:166
  682.2 42.8 %psum.47 = f32[1024]{0:T(1024)} all-reduce(f32[1024]{0:T(1024)S(1)} %bitcast.71), channel_id=1, replica_groups=mesh['fsdp'=8,'dp'=4] {'fsdp','dp'}, use_global_device_ids=true, to_apply=%region_24.25 | all-reduce | flops 1024 | bytes 8192 | tf_op jit(solution)/shard_map/psum | solution.py:183
  725.1 12.6 %add_convert_fusion = bf16[4096,1024]{1,0:T(8,128)(2,1)} fusion(bf16[4096,1024]{1,0:T(8,128)(2,1)} %param.12, s32[512]{0:T(512)S(1)} %copy-done.11, f32[512,1024]{1,0:T(8,128)S(1)} %get-tuple-element.28, f32[512,1024]{1,0:T(8,128)} %get-tuple-element.36, f32[1024]{0:T(1024)S(1)} %convert_element_type.137, f32[512]{0:T(512)S(1)} %get-tuple-element.25, ...), kind=kOutput, calls=%fused_computation | convolution fusion | flops 4316987392 | bytes 25190400 | tf_op jit(solution)/shard_map/kt,kd->td/dot_general | solution.py:162
  748.2 92.6 %all-reduce.7.cloned.1.call-done = (bf16[128,1024]{1,0:T(8,128)(2,1)}, bf16[128,4096]{1,0:T(8,128)(2,1)}, bf16[512,1024]{1,0:T(8,128)(2,1)}) async-done(((bf16[128,1024]{1,0:T(8,128)(2,1)}, bf16[128,4096]{1,0:T(8,128)(2,1)}, bf16[512,1024]{1,0:T(8,128)(2,1)}), (bf16[128,1024]{1,0:T(8,128)(2,1)}, bf16[128,4096]{1,0:T(8,128)(2,1)}, bf16[512,1024]{1,0:T(8,128)(2,1)})) %all-reduce.7.cloned.1.call-update) | async-done | bytes 2359312 | tf_op jit(solution)/shard_map/psum | solution.py:177
  (108 shorter events, 131.1 us)
Async XLA Ops:
  7.2 50.9 %all-gather.9.cloned.1.call-start = ((), (), s32[]{:S(2)}) async-start(), calls=%async_computation.4 | async-start | bytes 7077888 | tf_op jit(solution)/shard_map/all_gather | solution.py:51
  7.9 92.5 %all-gather.11.cloned.1.call-start = ((), (), s32[]{:S(2)}) async-start(), calls=%async_computation.5 | async-start | bytes 2359296 | tf_op jit(solution)/shard_map/all_gather | solution.py:52
  8.7 135.3 %all-gather.13.cloned.1.call-start = ((), (), s32[]{:S(2)}) async-start(), calls=%async_computation.6 | async-start | bytes 9437184 | tf_op jit(solution)/shard_map/all_gather | solution.py:57
  9.4 190.6 %all-gather.15.cloned.1.call-start = ((), (), s32[]{:S(2)}) async-start(), calls=%async_computation.7 | async-start | bytes 9437184 | tf_op jit(solution)/shard_map/all_gather | solution.py:58
  10.0 374.4 %reduce-scatter.5.cloned.1.call-start = ((), (), s32[]{:S(2)}) async-start(), calls=%async_computation.8 | async-start | bytes 14155776 | tf_op jit(solution)/shard_map/reduce_scatter | solution.py:171
  200.0 14.6 %copy-start.1 = (f32[512,1024]{1,0:T(8,128)S(1)}, f32[512,1024]{1,0:T(8,128)}, u32[]{:S(2)}) copy-start(f32[512,1024]{1,0:T(8,128)} %get-tuple-element.21) | copy-start | bytes 6291460
  214.6 10.9 %copy-start.2 = (f32[512,1024]{1,0:T(8,128)S(1)}, f32[512,1024]{1,0:T(8,128)}, u32[]{:S(2)}) copy-start(f32[512,1024]{1,0:T(8,128)} %get-tuple-element.31) | copy-start | bytes 6291460
  214.6 10.9 %copy-start.15 = (bf16[4096,1024]{1,0:T(8,128)(2,1)S(1)}, bf16[4096,1024]{1,0:T(8,128)(2,1)}, u32[]{:S(2)}) copy-start(bf16[4096,1024]{1,0:T(8,128)(2,1)} %all-gather.15.cloned.1.call-done) | copy-start | bytes 25165828
  214.6 10.9 %copy-start.19 = (f32[512,1024]{1,0:T(8,128)S(1)}, f32[512,1024]{1,0:T(8,128)}, u32[]{:S(2)}) copy-start(f32[512,1024]{1,0:T(8,128)} %fusion.12) | copy-start | bytes 6291460
  225.5 11.1 %copy-start.6 = (bf16[1024,1024]{1,0:T(8,128)(2,1)S(1)}, bf16[1024,1024]{1,0:T(8,128)(2,1)}, u32[]{:S(2)}) copy-start(bf16[1024,1024]{1,0:T(8,128)(2,1)} %all-gather.11.cloned.1.call-done) | copy-start | bytes 6291460
  241.2 10.6 %copy-start.8 = (bf16[512,1024]{0,1:T(8,128)(2,1)S(1)}, bf16[512,1024]{0,1:T(8,128)(2,1)}, u32[]{:S(2)}) copy-start(bf16[512,1024]{0,1:T(8,128)(2,1)} %copy.48) | copy-start | bytes 3145732
  241.2 10.6 %copy-start.9 = (bf16[512,1024]{0,1:T(8,128)(2,1)S(1)}, bf16[512,1024]{0,1:T(8,128)(2,1)}, u32[]{:S(2)}) copy-start(bf16[512,1024]{0,1:T(8,128)(2,1)} %copy.52) | copy-start | bytes 3145732
  251.8 29.4 %copy-start.16 = (bf16[16,64,512]{2,1,0:T(8,128)(2,1)}, bf16[16,64,512]{2,1,0:T(8,128)(2,1)S(1)}, u32[]{:S(2)}) copy-start(bf16[16,64,512]{2,1,0:T(8,128)(2,1)S(1)} %fusion.24) | copy-start | bytes 3145732
  264.6 12.4 %copy-start = (bf16[512,1024]{0,1:T(8,128)(2,1)S(1)}, bf16[512,1024]{0,1:T(8,128)(2,1)}, u32[]{:S(2)}) copy-start(bf16[512,1024]{0,1:T(8,128)(2,1)} %copy.49) | copy-start | bytes 3145732
  292.0 146.8 %reduce-scatter.7.cloned.1.call-start = ((), (), s32[]{:S(2)}) async-start(), calls=%async_computation.9 | async-start | bytes 4718592 | tf_op jit(solution)/shard_map/reduce_scatter | solution.py:172
  297.7 260.9 %reduce-scatter.11.cloned.1.call-start = ((), (), s32[]{:S(2)}) async-start(), calls=%async_computation.11 | async-start | bytes 18874368 | tf_op jit(solution)/shard_map/reduce_scatter | solution.py:167
  315.6 362.8 %reduce-scatter.9.cloned.1.call-start = ((), (), s32[]{:S(2)}) async-start(), calls=%async_computation.10 | async-start | bytes 18874368 | tf_op jit(solution)/shard_map/reduce_scatter | solution.py:166
  329.2 57.7 %copy-start.12 = (bf16[1024]{0:T(1024)(128)(2,1)S(1)}, bf16[1024]{0:T(1024)(128)(2,1)}, u32[]{:S(2)}) copy-start(bf16[1024]{0:T(1024)(128)(2,1)} %param.21) | copy-start | bytes 6148
  329.2 57.7 %copy-start.17 = (u32[32]{0:T(128)S(1)}, u32[32]{0:T(128)}, u32[]{:S(2)}) copy-start(u32[32]{0:T(128)} %constant.41) | copy-start | bytes 388
  329.2 59.0 %copy-start.4 = (bf16[16,64,512]{2,1,0:T(8,128)(2,1)S(1)}, bf16[16,64,512]{2,1,0:T(8,128)(2,1)}, u32[]{:S(2)}) copy-start(bf16[16,64,512]{2,1,0:T(8,128)(2,1)} %copy-done.3) | copy-start | bytes 3145732
  329.2 415.1 %all-gather.17.cloned.1.call-start = ((), (), s32[]{:S(2)}) async-start(), calls=%async_computation.12 | async-start | bytes 3932160 | tf_op jit(solution)/shard_map/all_gather | solution.py:176
  386.8 453.9 %all-reduce.7.cloned.1.call-start = ((), (), s32[]{:S(2)}) async-start(), calls=%async_computation.13 | async-start | bytes 4718592 | tf_op jit(solution)/shard_map/psum | solution.py:177
  388.2 34.3 %copy-start.11 = (s32[512]{0:T(512)S(1)}, s32[512]{0:T(512)}, u32[]{:S(2)}) copy-start(s32[512]{0:T(512)} %param.14) | copy-start | bytes 6148
  432.4 292.7 %copy-start.14 = (f32[512]{0:T(512)S(1)}, f32[512]{0:T(512)}, u32[]{:S(2)}) copy-start(f32[512]{0:T(512)} %copy-done.13) | copy-start | bytes 6148
  (6 other events, 13.2 us)
Sparse Core Ops, SparseCore 0:
  9.9 48.1 all-gather.8
  59.9 27.7 all-gather.10
  89.6 54.2 all-gather.12
  145.7 54.2 all-gather.14
  292.1 92.2 reduce-scatter.4
  387.6 51.1 reduce-scatter.6
  442.4 116.1 reduce-scatter.10
  562.2 116.1 reduce-scatter.8
  679.9 64.3 all-gather.16
  747.3 93.3 all-reduce.6
